TPU v7x, 256 devices: a whole 4x4x8 slice. The times are simulated.
256 devices in a mesh: space: 32 (over z, x), mode: 8 (over y, core).
Axes of the slice: x: 4, y: 4, z: 8, core: 2. Of those that a mesh axis runs over, the one named last changes fastest.
Arguments:
- vectors: float32 [55296, 256], P('space', 'mode'), may hold values from -6 to 6
- force_blocks: float32 [288, 27, 192, 192], P('space', None, 'mode'), as said below
- inverse_blocks: float32 [288, 192, 192], P('space'), as said below
- neighbours: int32 [288, 27], P('space'), may hold values from 0 to 287, as said below
Outputs:
- w_block: float32 [55296, 256], P('space', 'mode')
- hw_block: float32 [55296, 256], P('space', 'mode')
- gram_a: float32 [512, 2, 256], P(None, None, 'mode')
- gram_b: float32 [512, 2, 256], P(None, None, 'mode')
Inputs may be any that keep to these rules, and one draw needn't show every extreme that they name: `neighbours`: block rows are atom cells on a periodic grid of 32 layers of 3 x 3 cells; the rows of layer z are z * 9 to z * 9 + 8 in some order. Entry k = 9 (dz + 1) + 3 (dy + 1) + (dx + 1) of row i is the block row of the cell at offset (dz, dy, dx) from row i's cell, so entry 13 is i itself. H is symmetric: force_blocks[neighbours[i, k], 26 - k] is the transpose of force_blocks[i, k]. `inverse_blocks`: every block is symmetric.
All inputs are finite; a program needn't handle non-finite values.
Results may differ from a plain program's by a relative error of at most 0.00013.
Values sent between devices are 32-bit elements; how exact they have to be, the bound alone decides.
No kernel may reach another device: no remote copies, remote signals or barrier semaphores. Data moves between devices by JAX's collectives and lax.ppermute only.
A program may use at most 128 MiB of HBM per device.

v0:
```python
import jax
import jax.numpy as jnp
from jax import lax
from jax.sharding import PartitionSpec as P

CELLS = 9


def extended_2(block, sides, width):
    for axis, dim in sides:
        count = lax.axis_size(axis)
        forward = [(i, i + 1) for i in range(count - 1)]
        forward.append((count - 1, 0))
        backward = [(target, source) for source, target in forward]
        low = lax.ppermute(
            lax.slice_in_dim(block, block.shape[dim] - width, None, axis=dim), axis, forward
        )
        high = lax.ppermute(lax.slice_in_dim(block, 0, width, axis=dim), axis, backward)
        block = jnp.concatenate([low, block, high], axis=dim)
    return block


def apply_local(force_blocks, local_ids, extended):

    def accumulate(totals, offset):
        gathered = jnp.take(extended, local_ids[:, offset], axis=0)
        force_slice = lax.dynamic_index_in_dim(force_blocks, offset, 1, keepdims=False)
        product = jnp.einsum(
            "brc,bcm->brm",
            force_slice,
            gathered,
            precision=lax.Precision.HIGHEST,
            preferred_element_type=jnp.float32,
        )
        return (totals + product, None)

    initial = jnp.zeros(
        (force_blocks.shape[0], force_blocks.shape[2], extended.shape[2]), jnp.float32
    )
    totals, unused = lax.scan(
        accumulate, initial, jnp.arange(force_blocks.shape[1], dtype=jnp.int32)
    )
    regrouped = lax.all_to_all(totals, "mode", split_axis=2, concat_axis=1, tiled=True)
    return regrouped.reshape(-1, regrouped.shape[2])


def spread_search(search_field):
    gathered = lax.all_gather(search_field, "mode", axis=2, tiled=True)
    extended = extended_2(gathered, (("space", 0),), CELLS)
    return (gathered, extended)


def local_gram(flat_x, full_w, vectors, w_local, image_x, image_w, total_rows):
    basis = jnp.concatenate([flat_x, full_w.reshape(flat_x.shape)], axis=1)
    columns = jnp.stack([vectors, w_local, image_x, image_w], axis=1)
    return (
        jnp.einsum(
            "ra,rgj->agj",
            basis,
            columns,
            precision=lax.Precision.HIGHEST,
            preferred_element_type=jnp.float32,
        )
        / total_rows
    )


def local(vectors, force_blocks, inverse_blocks, neighbours):
    row_count, col_count = vectors.shape
    block_size = inverse_blocks.shape[1]
    block_rows = row_count // block_size
    slab_count = lax.axis_size("space")
    total_rows = row_count * slab_count
    own_layers = block_rows // CELLS
    layer_total = own_layers * slab_count
    slab_index = lax.axis_index("space")
    layer_of = neighbours // CELLS
    relative = (layer_of - slab_index * own_layers + 1) % layer_total
    local_ids = relative * CELLS + neighbours % CELLS
    stacked_x = vectors.reshape(block_rows, block_size, col_count)
    full_x = lax.all_gather(stacked_x, "mode", axis=2, tiled=True)
    extended_x = extended_2(full_x, (("space", 0),), CELLS)
    mode_count = full_x.shape[2]
    image_x = apply_local(force_blocks, local_ids, extended_x)
    flat_x = full_x.reshape(row_count, mode_count)
    rayleigh = lax.psum(
        jnp.einsum(
            "ra,rj->aj",
            flat_x,
            image_x,
            precision=lax.Precision.HIGHEST,
            preferred_element_type=jnp.float32,
        )
        / total_rows,
        "space",
    )
    residual = image_x - jnp.dot(
        flat_x, rayleigh, precision=lax.Precision.HIGHEST, preferred_element_type=jnp.float32
    )
    search_raw = jnp.einsum(
        "brc,bcm->brm",
        inverse_blocks,
        residual.reshape(block_rows, block_size, col_count),
        precision=lax.Precision.HIGHEST,
        preferred_element_type=jnp.float32,
    )
    squares = lax.psum(jnp.sum(search_raw * search_raw, axis=(0, 1)), "space")
    scales = lax.rsqrt(squares / total_rows + 1e-06)
    search_field = search_raw * scales
    full_w, extended_w = spread_search(search_field)
    hw_block = apply_local(force_blocks, local_ids, extended_w)
    w_block = search_field.reshape(row_count, col_count)
    gram_sum = lax.psum(
        local_gram(flat_x, full_w, vectors, w_block, image_x, hw_block, total_rows), "space"
    )
    gram_b = gram_sum[:, 0:2]
    gram_a = gram_sum[:, 2:4]
    return (w_block, hw_block, gram_a, gram_b)


def solution(mesh):
    in_specs = (
        P("space", "mode"),
        P("space", None, "mode", None),
        P("space", None, None),
        P("space", None),
    )
    out_specs = (
        P("space", "mode"),
        P("space", "mode"),
        P(None, None, "mode"),
        P(None, None, "mode"),
    )
    return jax.shard_map(local, mesh=mesh, in_specs=in_specs, out_specs=out_specs, check_vma=False)
```

profile of v0, /device:TPU:8, one launch (start us, length us, event | category | flops | bytes accessed | tf_op | source)
XLA Modules:
  0.0 1128.0 jit_solution(3499977427174082303)
XLA Ops:
  9.4 30.6 %all-gather.3.cloned.1.call-done = f32[9,192,256]{1,2,0:T(8,128)} async-done(((f32[9,192,32]{1,2,0:T(8,128)}), f32[9,192,256]{1,2,0:T(8,128)}) %all-gather.3.cloned.1.call-update) | async-done | bytes 1769488 | tf_op jit(solution)/shard_map/all_gather | solution.py:81
  42.0 5.5 collective-permute-start.1
  48.3 5.7 copy.80
  54.6 31.2 %collective-permute-done.1 = f32[9,192,256]{2,1,0:T(8,128)} collective-permute-done((f32[9,192,256]{2,1,0:T(8,128)S(1)}, f32[9,192,256]{2,1,0:T(8,128)}, u32[]{:S(2)}, u32[]{:S(2)}) %collective-permute-start.1) | collective-permute-done | bytes 1769504 | tf_op jit(solution)/shard_map/ppermute | solution.py:18
  94.4 5.2 pad_maximum_fusion
  99.6 7.6 copy.81
  107.2 248.9 %while.22 = (s32[]{:T(128)}, f32[9,24,256]{2,1,0:T(8,128)}, s32[27]{0:T(128)S(1)}, f32[9,27,24,192]{3,2,0,1:T(8,128)}, s32[9,27]{0,1:T(8,128)}, /*index=5*/f32[2...) while((s32[]{:T(128)}, f32[9,24,256]{2,1,0:T(8,128)}, s32[27]{0:T(128)S(1)}, ...), condition=%wide.region_1.3_spmd.clone, body=%wide.region_0.2_spmd.clone.sunk | while | flops 127956024 | bytes 5976391 | solution.py:40
  110.4 3.2 gather_fusion
  119.6 3.2 gather_fusion
  128.8 3.2 gather_fusion
  138.0 3.2 gather_fusion
  147.2 3.2 gather_fusion
  156.4 3.2 gather_fusion
  165.7 3.2 gather_fusion
  174.9 3.2 gather_fusion
  184.1 3.2 gather_fusion
  193.3 3.2 gather_fusion
  202.6 3.2 gather_fusion
  211.8 3.2 gather_fusion
  221.0 3.2 gather_fusion
  230.2 3.2 gather_fusion
  239.4 3.2 gather_fusion
  248.7 3.2 gather_fusion
  257.9 3.2 gather_fusion
  267.1 3.2 gather_fusion
  276.3 3.2 gather_fusion
  285.5 3.2 gather_fusion
  294.8 3.2 gather_fusion
  304.0 3.2 gather_fusion
  313.2 3.2 gather_fusion
  322.4 3.2 gather_fusion
  331.6 3.2 gather_fusion
  340.9 3.2 gather_fusion
  350.1 3.2 gather_fusion
  356.1 3.4 copy.82
  361.9 10.4 all_to_all.30
  375.9 3.5 copy.104
  384.2 141.0 %psum.21 = f32[256,32]{0,1:T(8,128)} all-reduce(f32[256,32]{0,1:T(8,128)} %fusion.27), channel_id=1, replica_groups=mesh['space'=32,'mode'=8] {'space'}, use_global_device_ids=true, to_apply=%region_2.4 | all-reduce | flops 8192 | bytes 65536 | tf_op jit(solution)/shard_map/psum | solution.py:86
  525.2 3.3 fusion.26
  530.4 3.6 multiply_reduce_fusion
  533.9 69.6 %psum.22 = f32[32]{0:T(128)S(1)} all-reduce(f32[32]{0:T(128)S(1)} %get-tuple-element.203), channel_id=1, replica_groups=mesh['space'=32,'mode'=8] {'space'}, use_global_device_ids=true, to_apply=%region_4.6 | all-reduce | flops 32 | bytes 256 | tf_op jit(solution)/shard_map/psum | solution.py:107
  605.4 25.1 %all-gather.5.cloned.1.call-done = f32[9,192,256]{1,2,0:T(8,128)} async-done(((f32[9,192,32]{1,2,0:T(8,128)}), f32[9,192,256]{1,2,0:T(8,128)}) %all-gather.5.cloned.1.call-update) | async-done | bytes 1769488 | tf_op jit(solution)/shard_map/all_gather | solution.py:48
  632.5 5.5 collective-permute-start.3
  638.1 38.3 %collective-permute-done.3 = f32[9,192,256]{2,1,0:T(8,128)} collective-permute-done((f32[9,192,256]{2,1,0:T(8,128)S(1)}, f32[9,192,256]{2,1,0:T(8,128)}, u32[]{:S(2)}, u32[]{:S(2)}) %collective-permute-start.3) | collective-permute-done | bytes 1769504 | tf_op jit(solution)/shard_map/ppermute | solution.py:18
  684.9 5.2 pad_maximum_fusion.1
  690.2 7.6 copy.92
  697.8 248.9 %while.23 = (s32[]{:T(128)}, f32[9,24,256]{2,1,0:T(8,128)}, s32[27]{0:T(128)S(1)}, f32[9,27,24,192]{3,2,0,1:T(8,128)}, s32[9,27]{0,1:T(8,128)}, /*index=5*/f32[2...) while((s32[]{:T(128)}, f32[9,24,256]{2,1,0:T(8,128)}, s32[27]{0:T(128)S(1)}, ...), condition=%wide.region_6.8_spmd.clone, body=%wide.region_5.7_spmd.clone.sunk | while | flops 127956024 | bytes 5976391 | solution.py:40
  701.0 3.2 gather_fusion.1
  710.1 3.2 gather_fusion.1
  719.3 3.2 gather_fusion.1
  728.6 3.2 gather_fusion.1
  737.8 3.2 gather_fusion.1
  747.0 3.2 gather_fusion.1
  756.2 3.2 gather_fusion.1
  765.4 3.2 gather_fusion.1
  774.7 3.2 gather_fusion.1
  783.9 3.2 gather_fusion.1
  830.0 3.2 gather_fusion.1
  857.7 3.2 gather_fusion.1
  931.4 3.2 gather_fusion.1
  946.6 3.5 copy.93
  953.3 5.4 all-to-all-start.1
  960.0 4.4 all-to-all-done.1
  980.4 139.4 %all-reduce.2.cloned.1.call-done = f32[512,4,32]{0,2,1:T(8,128)} async-done(((f32[512,4,32]{0,2,1:T(8,128)}), f32[512,4,32]{0,2,1:T(8,128)}) %all-reduce.2.cloned.1.call-update) | async-done | bytes 262160 | tf_op jit(solution)/shard_map/psum | solution.py:113
  (301 shorter events, 326.9 us)
Async XLA Ops:
  7.2 523.2 %copy-start = (f32[9,192,192]{2,1,0:T(8,128)S(1)}, f32[9,192,192]{2,1,0:T(8,128)}, u32[]{:S(2)}) copy-start(f32[9,192,192]{2,1,0:T(8,128)} %param.12) | copy-start | bytes 3981316
  7.2 32.8 %all-gather.3.cloned.1.call-start = ((), (), s32[]{:S(2)}) async-start(), calls=%async_computation.2 | async-start | bytes 2654208 | tf_op jit(solution)/shard_map/all_gather | solution.py:81
  9.3 621.2 %all-gather.5.cloned.1.call-start = ((), (), s32[]{:S(2)}) async-start(), calls=%async_computation.3 | async-start | bytes 2654208 | tf_op jit(solution)/shard_map/all_gather | solution.py:48
  42.0 12.0 %copy-start.2 = (f32[9,192,256]{2,1,0:T(8,128)}, f32[9,192,256]{2,1,0:T(8,128)S(1)}, u32[]{:S(2)}) copy-start(f32[9,192,256]{2,1,0:T(8,128)S(1)} %copy.76) | copy-start | bytes 5308420
  42.0 43.8 %collective-permute-start.1 = (f32[9,192,256]{2,1,0:T(8,128)S(1)}, f32[9,192,256]{2,1,0:T(8,128)}, u32[]{:S(2)}, u32[]{:S(2)}) collective-permute-start(f32[9,192,256]{2,1,0:T(8,128)S(1)} %copy.76), channel_id=1, source_target_pairs={{8,0},{16,8},{24,16},{32,24},{40,32},{48,40},{56,48},{64,56},{72,6... | collective-permute-start | bytes 5308424 | tf_op jit(solution)/shard_map/ppermute | solution.py:18
  47.5 43.9 %collective-permute-start = (f32[9,192,256]{2,1,0:T(8,128)S(1)}, f32[9,192,256]{2,1,0:T(8,128)}, u32[]{:S(2)}, u32[]{:S(2)}) collective-permute-start(f32[9,192,256]{2,1,0:T(8,128)S(1)} %copy.76), channel_id=1, source_target_pairs={{0,8},{8,16},{16,24},{24,32},{32,40},{40,48},{48,56},{56,64},{64,7... | collective-permute-start | bytes 5308424 | tf_op jit(solution)/shard_map/ppermute | solution.py:15
  375.9 5.8 copy-start.3
  632.5 52.4 %copy-start.7 = (f32[9,192,256]{2,1,0:T(8,128)}, f32[9,192,256]{2,1,0:T(8,128)S(1)}, u32[]{:S(2)}) copy-start(f32[9,192,256]{2,1,0:T(8,128)S(1)} %copy.87) | copy-start | bytes 5308420
  632.5 43.8 %collective-permute-start.3 = (f32[9,192,256]{2,1,0:T(8,128)S(1)}, f32[9,192,256]{2,1,0:T(8,128)}, u32[]{:S(2)}, u32[]{:S(2)}) collective-permute-start(f32[9,192,256]{2,1,0:T(8,128)S(1)} %copy.87), channel_id=1, source_target_pairs={{8,0},{16,8},{24,16},{32,24},{40,32},{48,40},{56,48},{64,56},{72,6... | collective-permute-start | bytes 5308424 | tf_op jit(solution)/shard_map/ppermute | solution.py:18
  638.1 43.9 %collective-permute-start.2 = (f32[9,192,256]{2,1,0:T(8,128)S(1)}, f32[9,192,256]{2,1,0:T(8,128)}, u32[]{:S(2)}, u32[]{:S(2)}) collective-permute-start(f32[9,192,256]{2,1,0:T(8,128)S(1)} %copy.87), channel_id=1, source_target_pairs={{0,8},{8,16},{16,24},{24,32},{32,40},{40,48},{48,56},{56,64},{64,7... | collective-permute-start | bytes 5308424 | tf_op jit(solution)/shard_map/ppermute | solution.py:15
  946.6 12.0 %copy-start.4 = (f32[9,24,8,32]{1,2,0,3:T(8,128)S(1)}, f32[9,24,8,32]{1,2,0,3:T(8,128)}, u32[]{:S(2)}) copy-start(f32[9,24,8,32]{1,2,0,3:T(8,128)} %copy.104) | copy-start | bytes 663556
  950.1 9.6 copy-start.10
  953.3 11.1 all-to-all-start.1
  958.7 161.1 %all-reduce.2.cloned.1.call-start = ((), (), s32[]{:S(2)}) async-start(), calls=%async_computation.4 | async-start | bytes 524288 | tf_op jit(solution)/shard_map/psum | solution.py:113
  959.9 8.5 copy-start.9
  968.4 4.4 copy-start.11
  970.7 1.0 copy-start.5
  972.8 1.7 copy-start.8
  974.5 147.0 %copy-start.1 = (f32[9,192,192]{2,1,0:T(8,128)S(1)}, f32[9,192,192]{2,1,0:T(8,128)}, u32[]{:S(2)}) copy-start(f32[9,192,192]{2,1,0:T(8,128)} %param.12) | copy-start | bytes 3981316
  976.7 2.6 copy-start.6
Sparse Core Ops, SparseCore 0:
  9.8 30.0 all-gather.2
  605.5 24.9 all-gather.4
  977.6 142.1 all-reduce.1
where the time goes:
time: 1140 us; the launch traced here: 1130 us
  local copies, waits for them, and re-layouts  277 us (24%)
  waiting for transfers between devices  274 us (24%)
  blocking collectives  221 us (19%)
  matrix products  163 us (14%)
  loops' own time  106 us (9%)
  other arithmetic  56.2 us (5%)
  starting transfers between devices  16.5 us (1%)
  between operations  13.9 us (1%)
    gather x54, local copies, waits for them, and re-layouts, accumulate(): gathered = jnp.take(extended, local_ids[:, offset], axis=0)  171 us
    dot_general x54, matrix products, accumulate(): jnp.einsum('brc,bcm->brm', force_slice, gathered, precision=lax.Precision...  152 us
    psum x1, blocking collectives, local(): lax.psum(jnp.einsum('ra,rj->aj', flat_x, image_x, precision=lax.Precision...  141 us
    psum x1, waiting for transfers between devices, local(): lax.psum(local_gram(flat_x, full_w, vectors, w_block, image_x, hw_block,...  139 us
    another operation x2, loops' own time, apply_local(): lax.scan(accumulate, initial, jnp.arange(force_blocks.shape[1], dtype=jnp...  106 us
    psum x1, blocking collectives, local(): squares = lax.psum(jnp.sum(search_raw * search_raw, axis=(0, 1)), 'space')  69.6 us
    ppermute x2, waiting for transfers between devices, extended_2(): lax.ppermute(lax.slice_in_dim(block, 0, width, axis=dim), axis, backward)  69.4 us
    and x54, other arithmetic, accumulate(): gathered = jnp.take(extended, local_ids[:, offset], axis=0)  37.9 us
  transfers between devices with their start and end apart: 8, of which 8 were waited for; matrix products, arithmetic and copies ran while one was open for 2% of the time, Pallas kernels for 0%

commit v1 on v0

--- a/solution.py
+++ b/solution.py
@@ -4,6 +4,24 @@
 from jax.sharding import PartitionSpec as P
 
 CELLS = 9
+
+
+def collect(shard, axis, dim):
+    ways, here, step = (lax.axis_size(axis), lax.axis_index(axis), shard.shape[dim])
+    lengths = [n * ways if d == dim else n for d, n in enumerate(shard.shape)]
+    full = lax.dynamic_update_slice_in_dim(
+        jnp.zeros(lengths, shard.dtype), shard, here * step, axis=dim
+    )
+    going_up = going_down = shard
+    for far in range(1, ways // 2 + 1):
+        going_up = lax.ppermute(going_up, axis, [(d, (d + 1) % ways) for d in range(ways)])
+        full = lax.dynamic_update_slice_in_dim(full, going_up, (here - far) % ways * step, axis=dim)
+        if 2 * far < ways:
+            going_down = lax.ppermute(going_down, axis, [(d, (d - 1) % ways) for d in range(ways)])
+            full = lax.dynamic_update_slice_in_dim(
+                full, going_down, (here + far) % ways * step, axis=dim
+            )
+    return full
 
 
 def extended_2(block, sides, width):
@@ -45,7 +63,7 @@
 
 
 def spread_search(search_field):
-    gathered = lax.all_gather(search_field, "mode", axis=2, tiled=True)
+    gathered = collect(search_field, "mode", 2)
     extended = extended_2(gathered, (("space", 0),), CELLS)
     return (gathered, extended)
 

time: 1140 us -> 1170 us (1.026)
  local copies, waits for them, and re-layouts: 277 us -> 322 us
    dynamic_update_slice x0 -> x8, local copies, waits for them, and re-layouts: none -> 43.7 us  [the longest x4 21.8 us: collect(): lax.dynamic_update_slice_in_dim(full, going_up, (here - far) % ways * ste...]
    all_gather x1 -> x0, waiting for transfers between devices: 25.1 us -> none  [spread_search(): gathered = lax.all_gather(search_field, 'mode', axis=2, tiled=True)]
    ppermute x0 -> x7, local copies, waits for them, and re-layouts: none -> 15.3 us  [the longest x4 8.75 us: collect(): lax.ppermute(going_up, axis, [(d, (d + 1) % ways) for d in range(ways)])]
    ppermute x0 -> x7, waiting for transfers between devices: none -> 12.6 us  [the longest x4 12.4 us: collect(): lax.ppermute(going_up, axis, [(d, (d + 1) % ways) for d in range(ways)])]
    unnamed x32 -> x37, local copies, waits for them, and re-layouts: 32.5 us -> 24.6 us
  transfers between devices with their start and end apart: 8 -> 14, of which waited for: 8 -> 11; matrix products, arithmetic and copies ran while one was open for 2% -> 6% of each run, Pallas kernels for 0% -> 0%
where the time goes in v1:
time: 1170 us
  local copies, waits for them, and re-layouts  322 us (28%)
  waiting for transfers between devices  264 us (23%)
  blocking collectives  221 us (19%)
  matrix products  165 us (14%)
  loops' own time  106 us (9%)
  other arithmetic  55.1 us (5%)
  starting transfers between devices  20.5 us (2%)
  between operations  14.3 us (1%)
    gather x54, local copies, waits for them, and re-layouts, accumulate(): gathered = jnp.take(extended, local_ids[:, offset], axis=0)  171 us
    dot_general x54, matrix products, accumulate(): jnp.einsum('brc,bcm->brm', force_slice, gathered, precision=lax.Precision...  152 us
    psum x1, blocking collectives, local(): lax.psum(jnp.einsum('ra,rj->aj', flat_x, image_x, precision=lax.Precision...  141 us
    psum x1, waiting for transfers between devices, local(): lax.psum(local_gram(flat_x, full_w, vectors, w_block, image_x, hw_block,...  139 us
    another operation x2, loops' own time, apply_local(): lax.scan(accumulate, initial, jnp.arange(force_blocks.shape[1], dtype=jnp...  106 us
    ppermute x2, waiting for transfers between devices, extended_2(): lax.ppermute(lax.slice_in_dim(block, 0, width, axis=dim), axis, backward)  69.7 us
    psum x1, blocking collectives, local(): squares = lax.psum(jnp.sum(search_raw * search_raw, axis=(0, 1)), 'space')  69.6 us
    and x54, other arithmetic, accumulate(): gathered = jnp.take(extended, local_ids[:, offset], axis=0)  37.9 us
  transfers between devices with their start and end apart: 14, of which 11 were waited for; matrix products, arithmetic and copies ran while one was open for 6% of the time, Pallas kernels for 0%

profile of v1, /device:TPU:8, one launch (start us, length us, event | category | flops | bytes accessed | tf_op | source)
XLA Modules:
  0.0 1166.7 jit_solution(7379699624365530440)
XLA Ops:
  9.3 30.6 %all-gather.2.cloned.1.call-done = f32[9,192,256]{1,2,0:T(8,128)} async-done(((f32[9,192,32]{1,2,0:T(8,128)}), f32[9,192,256]{1,2,0:T(8,128)}) %all-gather.2.cloned.1.call-update) | async-done | bytes 1769488 | tf_op jit(solution)/shard_map/all_gather | solution.py:99
  42.0 5.5 collective-permute-start.1
  48.3 5.7 copy.97
  54.7 31.1 %collective-permute-done.1 = f32[9,192,256]{2,1,0:T(8,128)} collective-permute-done((f32[9,192,256]{2,1,0:T(8,128)S(1)}, f32[9,192,256]{2,1,0:T(8,128)}, u32[]{:S(2)}, u32[]{:S(2)}) %collective-permute-start.1) | collective-permute-done | bytes 1769504 | tf_op jit(solution)/shard_map/ppermute | solution.py:36
  94.3 5.2 pad_maximum_fusion
  99.5 7.6 copy.98
  107.2 248.9 %while.22 = (s32[]{:T(128)}, f32[9,24,256]{2,1,0:T(8,128)}, s32[27]{0:T(128)S(1)}, f32[9,27,24,192]{3,2,0,1:T(8,128)}, s32[9,27]{0,1:T(8,128)}, /*index=5*/f32[2...) while((s32[]{:T(128)}, f32[9,24,256]{2,1,0:T(8,128)}, s32[27]{0:T(128)S(1)}, ...), condition=%wide.region_1.3_spmd.clone, body=%wide.region_0.2_spmd.clone.sunk | while | flops 127956024 | bytes 5976391 | solution.py:58
  110.4 3.2 gather_fusion
  119.5 3.2 gather_fusion
  128.7 3.2 gather_fusion
  137.9 3.2 gather_fusion
  147.2 3.2 gather_fusion
  156.4 3.2 gather_fusion
  165.6 3.2 gather_fusion
  174.8 3.2 gather_fusion
  184.1 3.2 gather_fusion
  193.3 3.2 gather_fusion
  202.5 3.2 gather_fusion
  211.7 3.2 gather_fusion
  220.9 3.2 gather_fusion
  230.2 3.2 gather_fusion
  239.4 3.2 gather_fusion
  248.6 3.2 gather_fusion
  257.8 3.2 gather_fusion
  267.0 3.2 gather_fusion
  276.3 3.2 gather_fusion
  285.5 3.2 gather_fusion
  294.7 3.2 gather_fusion
  303.9 3.2 gather_fusion
  313.1 3.2 gather_fusion
  322.4 3.2 gather_fusion
  356.0 3.4 copy.99
  361.8 10.4 all_to_all.30
  375.9 3.4 copy.123
  384.1 141.0 %psum.21 = f32[256,32]{0,1:T(8,128)} all-reduce(f32[256,32]{0,1:T(8,128)} %fusion.27), channel_id=1, replica_groups=mesh['space'=32,'mode'=8] {'space'}, use_global_device_ids=true, to_apply=%region_2.4 | all-reduce | flops 8192 | bytes 65536 | tf_op jit(solution)/shard_map/psum | solution.py:104
  525.1 3.3 fusion.26
  530.3 3.6 multiply_reduce_fusion
  533.8 69.6 %psum.22 = f32[32]{0:T(128)S(1)} all-reduce(f32[32]{0:T(128)S(1)} %get-tuple-element.203), channel_id=1, replica_groups=mesh['space'=32,'mode'=8] {'space'}, use_global_device_ids=true, to_apply=%region_4.6 | all-reduce | flops 32 | bytes 256 | tf_op jit(solution)/shard_map/psum | solution.py:125
  606.3 4.4 collective-permute-done.2
  612.7 4.1 collective-permute-done.4
  619.2 3.9 collective-permute-done.6
  624.5 6.1 dynamic_update_slice.24
  632.8 6.0 dynamic_update_slice.25
  641.0 6.0 dynamic_update_slice.26
  649.2 4.6 dynamic_update_slice.27
  656.0 4.2 dynamic_update_slice.28
  662.4 5.6 dynamic_update_slice.29
  670.2 5.6 dynamic_update_slice.30
  678.0 5.6 dynamic_update_slice.31
  686.1 38.6 %collective-permute-done.10 = f32[9,192,256]{2,1,0:T(8,128)} collective-permute-done((f32[9,192,256]{2,1,0:T(8,128)S(1)}, f32[9,192,256]{2,1,0:T(8,128)}, u32[]{:S(2)}, u32[]{:S(2)}) %collective-permute-start.10) | collective-permute-done | bytes 1769504 | tf_op jit(solution)/shard_map/ppermute | solution.py:36
  724.7 4.8 collective-permute-done.9
  729.4 4.9 pad_maximum_fusion.1
  734.4 248.9 %while.23 = (s32[]{:T(128)}, f32[9,24,256]{2,1,0:T(8,128)}, s32[27]{0:T(128)S(1)}, f32[9,27,24,192]{3,2,0,1:T(8,128)}, s32[9,27]{0,1:T(8,128)}, /*index=5*/f32[2...) while((s32[]{:T(128)}, f32[9,24,256]{2,1,0:T(8,128)}, s32[27]{0:T(128)S(1)}, ...), condition=%wide.region_6.8_spmd.clone, body=%wide.region_5.7_spmd.clone.sunk | while | flops 127956024 | bytes 5976391 | solution.py:58
  765.2 3.2 gather_fusion.1
  792.9 3.2 gather_fusion.1
  866.6 3.2 gather_fusion.1
  940.4 3.2 gather_fusion.1
  968.1 3.2 gather_fusion.1
  983.3 3.4 copy.113
  986.7 3.2 reshape.72
  989.9 6.5 all-to-all-start.1
  997.8 4.3 all-to-all-done.1
  1011.6 3.8 fusion.22
  1019.1 139.1 %all-reduce.2.cloned.1.call-done = f32[512,4,32]{0,2,1:T(8,128)} async-done(((f32[512,4,32]{0,2,1:T(8,128)}), f32[512,4,32]{0,2,1:T(8,128)}) %all-reduce.2.cloned.1.call-update) | async-done | bytes 262160 | tf_op jit(solution)/shard_map/psum | solution.py:131
  (331 shorter events, 369.7 us)
Async XLA Ops:
  7.2 523.1 %copy-start = (f32[9,192,192]{2,1,0:T(8,128)S(1)}, f32[9,192,192]{2,1,0:T(8,128)}, u32[]{:S(2)}) copy-start(f32[9,192,192]{2,1,0:T(8,128)} %param.12) | copy-start | bytes 3981316
  7.2 32.8 %all-gather.2.cloned.1.call-start = ((), (), s32[]{:S(2)}) async-start(), calls=%async_computation.2 | async-start | bytes 2654208 | tf_op jit(solution)/shard_map/all_gather | solution.py:99
  42.0 12.0 %copy-start.2 = (f32[9,192,256]{2,1,0:T(8,128)}, f32[9,192,256]{2,1,0:T(8,128)S(1)}, u32[]{:S(2)}) copy-start(f32[9,192,256]{2,1,0:T(8,128)S(1)} %copy.93) | copy-start | bytes 5308420
  42.0 43.8 %collective-permute-start.1 = (f32[9,192,256]{2,1,0:T(8,128)S(1)}, f32[9,192,256]{2,1,0:T(8,128)}, u32[]{:S(2)}, u32[]{:S(2)}) collective-permute-start(f32[9,192,256]{2,1,0:T(8,128)S(1)} %copy.93), channel_id=1, source_target_pairs={{8,0},{16,8},{24,16},{32,24},{40,32},{48,40},{56,48},{64,56},{72,6... | collective-permute-start | bytes 5308424 | tf_op jit(solution)/shard_map/ppermute | solution.py:36
  47.5 43.9 %collective-permute-start = (f32[9,192,256]{2,1,0:T(8,128)S(1)}, f32[9,192,256]{2,1,0:T(8,128)}, u32[]{:S(2)}, u32[]{:S(2)}) collective-permute-start(f32[9,192,256]{2,1,0:T(8,128)S(1)} %copy.93), channel_id=1, source_target_pairs={{0,8},{8,16},{16,24},{24,32},{32,40},{40,48},{48,56},{56,64},{64,7... | collective-permute-start | bytes 5308424 | tf_op jit(solution)/shard_map/ppermute | solution.py:33
  375.9 5.7 copy-start.3
  604.5 18.6 %copy-start.9 = (f32[9,192,32]{1,2,0:T(8,128)}, f32[9,192,32]{1,2,0:T(8,128)S(1)}, u32[]{:S(2)}) copy-start(f32[9,192,32]{1,2,0:T(8,128)S(1)} %multiply_bitcast_fusion) | copy-start | bytes 663556
  604.5 6.2 collective-permute-start.2
  604.6 6.1 collective-permute-start.3
  610.7 12.4 %copy-start.14 = (f32[9,192,32]{1,2,0:T(8,128)}, f32[9,192,32]{1,2,0:T(8,128)S(1)}, u32[]{:S(2)}) copy-start(f32[9,192,32]{1,2,0:T(8,128)S(1)} %collective-permute-done.2) | copy-start | bytes 663556
  610.7 6.1 collective-permute-start.4
  610.7 12.4 %copy-start.12 = (f32[9,192,32]{1,2,0:T(8,128)}, f32[9,192,32]{1,2,0:T(8,128)S(1)}, u32[]{:S(2)}) copy-start(f32[9,192,32]{1,2,0:T(8,128)S(1)} %collective-permute-done.3) | copy-start | bytes 663556
  610.7 6.3 collective-permute-start.5
  616.8 6.3 copy-start.13
  616.8 6.3 collective-permute-start.6
  617.0 51.0 %collective-permute-start.7 = (f32[9,192,32]{1,2,0:T(8,128)}, f32[9,192,32]{1,2,0:T(8,128)}, u32[]{:S(2)}, u32[]{:S(2)}) collective-permute-start(f32[9,192,32]{1,2,0:T(8,128)} %collective-permute-done.5), channel_id=1, source_target_pairs={{0,7},{1,0},{2,1},{3,2},{4,3},{5,4},{6,5},{7,6},{8,15},{9,8},{10,9... | collective-permute-start | bytes 663560 | tf_op jit(solution)/shard_map/ppermute | solution.py:20
  623.1 52.7 %collective-permute-start.8 = (f32[9,192,32]{1,2,0:T(8,128)}, f32[9,192,32]{1,2,0:T(8,128)}, u32[]{:S(2)}, u32[]{:S(2)}) collective-permute-start(f32[9,192,32]{1,2,0:T(8,128)} %collective-permute-done.6), channel_id=1, source_target_pairs={{0,1},{1,2},{2,3},{3,4},{4,5},{5,6},{6,7},{7,0},{8,9},{9,10},{10,1... | collective-permute-start | bytes 663560 | tf_op jit(solution)/shard_map/ppermute | solution.py:17
  683.6 50.7 %copy-start.4 = (f32[9,192,256]{2,1,0:T(8,128)}, f32[9,192,256]{2,1,0:T(8,128)S(1)}, u32[]{:S(2)}) copy-start(f32[9,192,256]{2,1,0:T(8,128)S(1)} %dynamic_update_slice.31) | copy-start | bytes 5308420
  683.7 41.0 %collective-permute-start.10 = (f32[9,192,256]{2,1,0:T(8,128)S(1)}, f32[9,192,256]{2,1,0:T(8,128)}, u32[]{:S(2)}, u32[]{:S(2)}) collective-permute-start(f32[9,192,256]{2,1,0:T(8,128)S(1)} %dynamic_update_slice.31), channel_id=1, source_target_pairs={{8,0},{16,8},{24,16},{32,24},{40,32},{48,40},{56,48},{64,56},{72,6... | collective-permute-start | bytes 5308424 | tf_op jit(solution)/shard_map/ppermute | solution.py:36
  685.7 43.7 %collective-permute-start.9 = (f32[9,192,256]{2,1,0:T(8,128)S(1)}, f32[9,192,256]{2,1,0:T(8,128)}, u32[]{:S(2)}, u32[]{:S(2)}) collective-permute-start(f32[9,192,256]{2,1,0:T(8,128)S(1)} %dynamic_update_slice.31), channel_id=1, source_target_pairs={{0,8},{8,16},{16,24},{24,32},{32,40},{40,48},{48,56},{56,64},{64,7... | collective-permute-start | bytes 5308424 | tf_op jit(solution)/shard_map/ppermute | solution.py:33
  986.6 9.7 copy-start.5
  986.7 10.8 copy-start.10
  989.9 12.3 %all-to-all-start.1 = ((f32[8,1,6912]{2,1,0:T(1,128)}), f32[8,1,6912]{2,1,0:T(1,128)}, u32[]{:S(2)}, u32[]{:S(2)}) async-start(f32[8,1,6912]{2,1,0:T(1,128)} %reshape.72), calls=%async_computation.1 | async-start | bytes 442368 | tf_op jit(solution)/shard_map/all_to_all | solution.py:61
  996.4 161.8 %all-reduce.2.cloned.1.call-start = ((), (), s32[]{:S(2)}) async-start(), calls=%async_computation.3 | async-start | bytes 524288 | tf_op jit(solution)/shard_map/psum | solution.py:131
  997.6 8.5 copy-start.8
  1006.1 4.4 copy-start.11
  1008.4 1.0 copy-start.6
  1011.6 148.2 %copy-start.1 = (f32[9,192,192]{2,1,0:T(8,128)S(1)}, f32[9,192,192]{2,1,0:T(8,128)}, u32[]{:S(2)}) copy-start(f32[9,192,192]{2,1,0:T(8,128)} %param.12) | copy-start | bytes 3981316
  1015.4 2.6 copy-start.7
Sparse Core Ops, SparseCore 0:
  9.8 30.0 all-gather.1
  1016.3 141.8 all-reduce.1
